TPU v7x, 512 devices: a whole 4x4x16 slice. The times are simulated.
512 devices in a mesh: req: 64 (over y_hi, z, core), tp: 8 (over y_lo, x).
Axes of the slice: x: 4, y: 4 (y_hi: 2, y_lo: 2; y = y_hi * 2 + y_lo), z: 16, core: 2. Of those that a mesh axis runs over, the one named last changes fastest.
Arguments:
- tokens: bfloat16 [64, 512, 2048], P('req', 'tp'), may hold values from -6 to 6
- w_q: bfloat16 [2048, 1024], P(None, 'tp')
- w_k: bfloat16 [2048, 1024], P(None, 'tp')
- w_v: bfloat16 [2048, 1024], P(None, 'tp'), may hold values from -0.125 to 0.125
- w_o: bfloat16 [1024, 2048], P('tp'), may hold values from -0.1875 to 0.1875
- q_gain: float32 [1024], P('tp'), may hold values from 0.1 to 1.9
- k_gain: float32 [1024], P('tp'), may hold values from 0.1 to 1.9
- out_gain: float32 [2048], replicated, may hold values from 0.1 to 1.9
- cache_lens: int32 [64], P('req'), may hold values from 512 to 4096, as said below
- group_ids: int32 [64], replicated, may hold values from 0 to 7
- prefix_cache: bfloat16 [8, 1024, 2048], P(None, 'req', 'tp'), may hold values from -6 to 6
- cache_rows: bfloat16 [64, 4096, 2048], P('req', None, 'tp'), may hold values from -105 to 105
Outputs:
- hidden: bfloat16 [64, 512, 2048], P('req', 'tp')
- appended: bfloat16 [64, 512, 2048], P('req', None, 'tp')
Inputs may be any that keep to these rules, and one draw needn't show every extreme that they name: `cache_lens`: every draw holds a request with exactly 4096 cached positions.
All inputs are finite; a program needn't handle non-finite values.
Results may differ from a plain program's by a relative error of at most 0.013.
Values may be sent and summed in bfloat16 or wider, within the bound.
No kernel may reach another device: no remote copies, remote signals or barrier semaphores. Data moves between devices by JAX's collectives and lax.ppermute only.
A program may use at most 64 MiB of HBM per device.

v0:
```python
import jax
import jax.numpy as jnp
from jax import lax
from jax.sharding import PartitionSpec as P

HEADS = 8
HD = 128
NEW = 512


def rotate(values_in, positions):
    half_dim = values_in.shape[-1] // 2
    exponent = jnp.arange(half_dim, dtype=jnp.float32) * (-2.0 / values_in.shape[-1])
    inverse = jnp.power(jnp.float32(500000.0), exponent)
    angles = positions[:, None] * inverse[None, :]
    cosine = jnp.cos(angles)[:, None, :]
    sine_part = jnp.sin(angles)[:, None, :]
    first_half = values_in[..., :half_dim]
    second_half = values_in[..., half_dim:]
    return jnp.concatenate(
        [
            first_half * cosine - second_half * sine_part,
            second_half * cosine + first_half * sine_part,
        ],
        -1,
    )


def rms_scale(values_in, gain_vector):
    mean_sq = jnp.mean(values_in * values_in, axis=-1, keepdims=True)
    return values_in * lax.rsqrt(mean_sq + 1e-06) * gain_vector


def absorb(state_now, queries, keys_block, values_block, visible):
    running_max, denominator, weighted = state_now
    scores = jnp.einsum(
        "hqd,khd->hqk", queries, keys_block, preferred_element_type=jnp.float32
    ) * HD ** (-0.5)
    scores = jnp.where(visible[None], scores, -1e30)
    updated = jnp.maximum(running_max, jnp.max(scores, -1))
    factor = jnp.exp(running_max - updated)
    weights = jnp.where(visible[None], jnp.exp(scores - updated[..., None]), 0.0)
    denominator = denominator * factor + jnp.sum(weights, -1)
    weighted = weighted * factor[..., None] + jnp.einsum(
        "hqk,khd->hqd",
        weights.astype(jnp.bfloat16),
        values_block,
        preferred_element_type=jnp.float32,
    )
    return (updated, denominator, weighted)


def per_device(
    tokens,
    w_q,
    w_k,
    w_v,
    w_o,
    q_gain,
    k_gain,
    out_gain,
    cache_lens,
    group_ids,
    prefix_cache,
    cache_rows,
):
    heads_local = w_q.shape[1] // HD
    width_local = heads_local * HD
    flat_rows = lax.all_gather(tokens, "tp", axis=1, tiled=True)[0]
    projected = jnp.concatenate(
        [
            jnp.dot(flat_rows, w_q, preferred_element_type=jnp.float32)[None],
            jnp.dot(flat_rows, w_k, preferred_element_type=jnp.float32)[None],
            jnp.dot(flat_rows, w_v, preferred_element_type=jnp.float32)[None],
        ],
        axis=2,
    )[0]
    queries = projected[:, :width_local]
    keys_new = projected[:, width_local : 2 * width_local]
    values_new = projected[:, 2 * width_local :]
    square_sums = lax.psum((jnp.sum(queries * queries, -1), jnp.sum(keys_new * keys_new, -1)), "tp")
    full_width = HEADS * HD
    queries = queries * lax.rsqrt(square_sums[0] / full_width + 1e-06)[:, None] * q_gain
    keys_new = keys_new * lax.rsqrt(square_sums[1] / full_width + 1e-06)[:, None] * k_gain
    prefix_len = prefix_cache.shape[1] * lax.axis_size("req")
    length = cache_lens[0]
    positions = (prefix_len + length + jnp.arange(NEW, dtype=jnp.int32)).astype(jnp.float32)
    q_rot = rotate(queries.reshape(NEW, heads_local, HD), positions).astype(jnp.bfloat16)
    k_rot = rotate(keys_new.reshape(NEW, heads_local, HD), positions).astype(jnp.bfloat16)
    v_new = values_new.reshape(NEW, heads_local, HD).astype(jnp.bfloat16)
    appended = jnp.stack([k_rot, v_new], axis=2).reshape(1, NEW, heads_local * 2 * HD)
    q_heads = jnp.transpose(q_rot, (1, 0, 2))
    state_now = (
        jnp.full((heads_local, NEW), -1e30, jnp.float32),
        jnp.zeros((heads_local, NEW), jnp.float32),
        jnp.zeros((heads_local, NEW, HD), jnp.float32),
    )
    row_ids = jnp.arange(NEW, dtype=jnp.int32)
    state_now = absorb(state_now, q_heads, k_rot, v_new, row_ids[None, :] <= row_ids[:, None])
    cached = cache_rows[0]
    key_block = min(512, cached.shape[0])

    def cache_step(block_index, state_in):
        block = lax.dynamic_slice_in_dim(cached, block_index * key_block, key_block, 0).reshape(
            key_block, heads_local, 2, HD
        )
        columns = block_index * key_block + jnp.arange(key_block, dtype=jnp.int32)
        visible = jnp.broadcast_to(columns[None, :] < length, (NEW, key_block))
        return absorb(state_in, q_heads, block[:, :, 0], block[:, :, 1], visible)

    block_count = cached.shape[0] // key_block
    state_now = lax.fori_loop(0, block_count, cache_step, state_now)
    group_id = group_ids[lax.axis_index("req")]
    chosen = lax.dynamic_index_in_dim(
        lax.all_gather(prefix_cache, "req", axis=1, tiled=True), group_id, 0, keepdims=False
    )
    count = chosen.shape[0]
    chosen = chosen.reshape(count, heads_local, 2, HD)
    state_now = absorb(
        state_now, q_heads, chosen[:, :, 0], chosen[:, :, 1], jnp.ones((NEW, count), dtype=bool)
    )
    running_max, denominator, weighted = state_now
    attended = (
        jnp.transpose(weighted / denominator[..., None], (1, 0, 2))
        .reshape(NEW, width_local)
        .astype(jnp.bfloat16)
    )
    partial_out = jnp.dot(attended, w_o, preferred_element_type=jnp.float32)
    share_rows = tokens.shape[1]
    summed = lax.psum(partial_out.astype(jnp.bfloat16), "tp").astype(jnp.float32)
    mine = lax.dynamic_slice_in_dim(summed, lax.axis_index("tp") * share_rows, share_rows, 0)
    hidden = (tokens[0].astype(jnp.float32) + rms_scale(mine, out_gain)).astype(jnp.bfloat16)[None]
    return (hidden, appended)


def solution(mesh):
    return jax.shard_map(
        per_device,
        mesh=mesh,
        in_specs=(
            P("req", "tp", None),
            P(None, "tp"),
            P(None, "tp"),
            P(None, "tp"),
            P("tp", None),
            P("tp"),
            P("tp"),
            P(),
            P("req"),
            P(),
            P(None, "req", "tp"),
            P("req", None, "tp"),
        ),
        out_specs=(P("req", "tp", None), P("req", None, "tp")),
        check_vma=False,
    )
```

profile of v0, /device:TPU:32, one launch (start us, length us, event | category | flops | bytes accessed | tf_op | source)
XLA Modules:
  0.0 328.0 jit_solution(8489403628430038322)
XLA Ops:
  7.2 0.7 all-gather.3.cloned.1.call-update
  8.0 1.5 copy.30
  10.2 3.0 copy.28
  15.8 47.3 %all-gather.3.cloned.1.call-done = bf16[1,512,2048]{2,1,0:T(8,128)(2,1)} async-done(((bf16[1,64,2048]{2,1,0:T(8,128)(2,1)}), bf16[1,512,2048]{2,1,0:T(8,128)(2,1)}) %all-gather.3.cloned.1.call-update) | async-done | bytes 2097168 | tf_op jit(solution)/shard_map/all_gather | solution.py:69
  63.1 2.6 fusion.19
  65.7 0.8 fusion.22
  66.7 0.8 fusion.25
  67.7 17.2 %all-reduce = (f32[512]{0:T(512)S(1)}, f32[512]{0:T(512)S(1)}) all-reduce(f32[512]{0:T(512)S(1)} %get-tuple-element.168, f32[512]{0:T(512)S(1)} %get-tuple-element.167), channel_id=1, replica_groups=mesh['req'=64,'tp'=8] {'tp'}, use_global_device_ids=true, to_apply=%region_1.0 | all-reduce | flops 1024 | bytes 8192 | tf_op jit(solution)/shard_map/psum | solution.py:81
  85.0 1.3 fusion.63
  86.9 1.5 pad_maximum_fusion.2
  88.4 1.0 copy.29
  89.4 1.3 fusion.78
  90.9 1.3 fusion.28
  92.2 15.0 %while.17 = (s32[]{:T(128)}, f32[1,512]{1,0:T(1,128)S(1)}, f32[1,512]{1,0:T(1,128)S(1)}, f32[1,512,128]{2,1,0:T(8,128)S(1)}, s32[]{:T(128)}, /*index=5*/bf16[409...) while((s32[]{:T(128)}, f32[1,512]{1,0:T(1,128)S(1)}, ...), condition=%wide.region_9.10_spmd, body=%wide.region_6.9_spmd.sunk | while | flops 136710144 | bytes 4622503 | solution.py:112
  107.2 110.1 %all-gather.5.cloned.1.call-done = bf16[8,1024,256]{2,0,1:T(8,128)(2,1)} async-done(((bf16[8,16,256]{2,0,1:T(8,128)(2,1)}), bf16[8,1024,256]{2,0,1:T(8,128)(2,1)}) %all-gather.5.cloned.1.call-update) | async-done | bytes 4194320 | tf_op jit(solution)/shard_map/all_gather | solution.py:115
  217.3 3.3 constant_dynamic-slice_fusion.1
  220.5 1.3 copy.35
  221.9 1.4 multiply_reduce_fusion
  223.8 2.4 convolution_convert_fusion
  226.3 1.0 fusion.71
  227.3 0.8 copy.34
  228.2 90.3 %all-reduce.3.cloned.1.call-done = bf16[512,2048]{1,0:T(8,128)(2,1)} async-done(((bf16[512,2048]{1,0:T(8,128)(2,1)}), bf16[512,2048]{1,0:T(8,128)(2,1)}) %all-reduce.3.cloned.1.call-update) | async-done | bytes 2097168 | tf_op jit(solution)/shard_map/psum | solution.py:130
  318.5 1.1 fusion.43
  319.6 1.8 fusion.47
  (114 shorter events, 17.1 us)
Async XLA Ops:
  7.2 216.6 %copy-start = (bf16[128,2048]{1,0:T(8,128)(2,1)S(1)}, bf16[128,2048]{1,0:T(8,128)(2,1)}, u32[]{:S(2)}) copy-start(bf16[128,2048]{1,0:T(8,128)(2,1)} %param.18) | copy-start | bytes 1572868
  7.2 55.9 %all-gather.3.cloned.1.call-start = ((), (), s32[]{:S(2)}) async-start(), calls=%async_computation | async-start | bytes 2359296 | tf_op jit(solution)/shard_map/all_gather | solution.py:69
  7.9 209.3 %all-gather.5.cloned.1.call-start = ((), (), s32[]{:S(2)}) async-start(), calls=%async_computation.1 | async-start | bytes 4259840 | tf_op jit(solution)/shard_map/all_gather | solution.py:115
  9.5 309.0 %all-reduce.3.cloned.1.call-start = ((), (), s32[]{:S(2)}) async-start(), calls=%async_computation.2 | async-start | bytes 4194304 | tf_op jit(solution)/shard_map/psum | solution.py:130
  10.2 3.0 copy-start.14
  10.2 52.8 %copy-start.6 = (bf16[2048,128]{1,0:T(8,128)(2,1)S(1)}, bf16[2048,128]{1,0:T(8,128)(2,1)}, u32[]{:S(2)}) copy-start(bf16[2048,128]{1,0:T(8,128)(2,1)} %param.15) | copy-start | bytes 1572868
  63.1 2.6 copy-start.1
  63.1 2.6 copy-start.7
  65.7 1.0 copy-start.8
  66.7 18.2 %copy-start.12 = (f32[128]{0:T(128)S(1)}, f32[128]{0:T(128)}, u32[]{:S(2)}) copy-start(f32[128]{0:T(128)} %param.20) | copy-start | bytes 1540
  66.7 18.2 %copy-start.13 = (f32[128]{0:T(128)S(1)}, f32[128]{0:T(128)}, u32[]{:S(2)}) copy-start(f32[128]{0:T(128)} %param.19) | copy-start | bytes 1540
  67.6 23.1 %copy-start.2 = (f32[512,384]{0,1:T(8,128)}, f32[512,384]{0,1:T(8,128)S(1)}, u32[]{:S(2)}) copy-start(f32[512,384]{0,1:T(8,128)S(1)} %maximum_bitcast_fusion) | copy-start | bytes 2359300
  86.2 0.6 copy-start.4
  107.2 114.7 %copy-start.5 = (bf16[512,1,64]{0,2,1:T(8,128)(2,1)S(1)}, bf16[512,1,64]{0,2,1:T(8,128)(2,1)}, u32[]{:S(2)}) copy-start(bf16[512,1,64]{0,2,1:T(8,128)(2,1)} %copy-done.4) | copy-start | bytes 196612
  226.2 1.1 copy-start.9
  226.2 1.1 copy-start.10
  226.2 93.4 %copy-start.3 = (bf16[1,64,2048]{2,1,0:T(8,128)(2,1)S(1)}, bf16[1,64,2048]{2,1,0:T(8,128)(2,1)}, u32[]{:S(2)}) copy-start(bf16[1,64,2048]{2,1,0:T(8,128)(2,1)} %param.14) | copy-start | bytes 786436
  226.2 93.4 %copy-start.11 = (f32[2048]{0:T(1024)S(1)}, f32[2048]{0:T(1024)}, u32[]{:S(2)}) copy-start(f32[2048]{0:T(1024)} %param.21) | copy-start | bytes 24580
Sparse Core Ops, SparseCore 0:
  10.1 52.9 all-gather.2
  66.9 150.2 all-gather.4
  226.4 92.0 all-reduce.2
where the time goes:
time: 329 us; the launch traced here: 328 us
  waiting for transfers between devices  248 us (75%)
  matrix products  17.8 us (5%)
  blocking collectives  17.2 us (5%)
  between operations  16.6 us (5%)
  other arithmetic  13.8 us (4%)
  local copies, waits for them, and re-layouts  13.6 us (4%)
    all_gather x1, waiting for transfers between devices, per_device(): lax.all_gather(prefix_cache, 'req', axis=1, tiled=True)  110 us
    psum x1, waiting for transfers between devices, per_device(): lax.psum(partial_out.astype(jnp.bfloat16), 'tp').astype(jnp.float32)  90.3 us
    all_gather x1, waiting for transfers between devices, per_device(): flat_rows = lax.all_gather(tokens, 'tp', axis=1, tiled=True)[0]  47.3 us
    psum x1, blocking collectives, per_device(): lax.psum((jnp.sum(queries * queries, -1), jnp.sum(keys_new * keys_new, -1...  17.2 us
    unnamed x34, local copies, waits for them, and re-layouts  7.52 us
  transfers between devices with their start and end apart: 3, of which 3 were waited for; matrix products, arithmetic and copies ran while one was open for 10% of the time, Pallas kernels for 0%

commit v1 on v0

--- a/solution.py
+++ b/solution.py
@@ -2,6 +2,7 @@
 import jax.numpy as jnp
 from jax import lax
 from jax.sharding import PartitionSpec as P
+from jax.lax import all_gather
 
 HEADS = 8
 HD = 128
@@ -64,6 +65,10 @@
     prefix_cache,
     cache_rows,
 ):
+
+    def recast_slot(row_data, lane_axis):
+        return all_gather(row_data, lane_axis).sum(axis=0)
+
     heads_local = w_q.shape[1] // HD
     width_local = heads_local * HD
     flat_rows = lax.all_gather(tokens, "tp", axis=1, tiled=True)[0]
@@ -127,7 +132,7 @@
     )
     partial_out = jnp.dot(attended, w_o, preferred_element_type=jnp.float32)
     share_rows = tokens.shape[1]
-    summed = lax.psum(partial_out.astype(jnp.bfloat16), "tp").astype(jnp.float32)
+    summed = recast_slot(partial_out.astype(jnp.bfloat16), "tp").astype(jnp.float32)
     mine = lax.dynamic_slice_in_dim(summed, lax.axis_index("tp") * share_rows, share_rows, 0)
     hidden = (tokens[0].astype(jnp.float32) + rms_scale(mine, out_gain)).astype(jnp.bfloat16)[None]
     return (hidden, appended)

time: 329 us -> 417 us (1.27)
  the two profiles are of different devices: /device:TPU:32 before, /device:TPU:1 now
where the time goes in v1:
time: 417 us; the launch traced here: 416 us
  waiting for transfers between devices  332 us (80%)
  other arithmetic  20.5 us (5%)
  matrix products  16.9 us (4%)
  between operations  16.6 us (4%)
  blocking collectives  14.7 us (4%)
  local copies, waits for them, and re-layouts  14.3 us (3%)
    all_gather x1, waiting for transfers between devices, recast_slot(): return all_gather(row_data, lane_axis).sum(axis=0)  170 us
    all_gather x1, waiting for transfers between devices, per_device(): lax.all_gather(prefix_cache, 'req', axis=1, tiled=True)  119 us
    all_gather x1, waiting for transfers between devices, per_device(): flat_rows = lax.all_gather(tokens, 'tp', axis=1, tiled=True)[0]  42.5 us
    psum x1, blocking collectives, per_device(): lax.psum((jnp.sum(queries * queries, -1), jnp.sum(keys_new * keys_new, -1...  14.7 us
    reduce_sum x1, other arithmetic, recast_slot(): return all_gather(row_data, lane_axis).sum(axis=0)  9.45 us
  transfers between devices with their start and end apart: 3, of which 3 were waited for; matrix products, arithmetic and copies ran while one was open for 8% of the time, Pallas kernels for 0%

profile of v1, /device:TPU:1, one launch (start us, length us, event | category | flops | bytes accessed | tf_op | source)
XLA Modules:
  0.0 416.1 jit_solution(11173976604058768245)
XLA Ops:
  7.2 0.7 all-gather.5.cloned.1.call-update
  8.0 1.5 copy.30
  10.2 1.2 dynamic_slice.17
  12.8 3.0 copy.28
  16.4 42.5 %all-gather.5.cloned.1.call-done = bf16[1,512,2048]{2,1,0:T(8,128)(2,1)} async-done(((bf16[1,64,2048]{2,1,0:T(8,128)(2,1)}), bf16[1,512,2048]{2,1,0:T(8,128)(2,1)}) %all-gather.5.cloned.1.call-update) | async-done | bytes 2097168 | tf_op jit(solution)/shard_map/all_gather | solution.py:74
  58.9 2.6 fusion.22
  61.5 0.8 fusion.25
  62.6 0.8 fusion.19
  63.5 14.7 %all-reduce = (f32[512]{0:T(512)S(1)}, f32[512]{0:T(512)S(1)}) all-reduce(f32[512]{0:T(512)S(1)} %get-tuple-element.168, f32[512]{0:T(512)S(1)} %get-tuple-element.167), channel_id=1, replica_groups=mesh['req'=64,'tp'=8] {'tp'}, use_global_device_ids=true, to_apply=%region_1.0 | all-reduce | flops 1024 | bytes 8192 | tf_op jit(solution)/shard_map/psum | solution.py:86
  78.4 1.3 fusion.63
  80.3 0.7 pad_maximum_fusion.2
  80.9 1.0 copy.29
  82.0 1.3 fusion.78
  83.5 1.3 fusion.28
  84.7 15.0 %while.17 = (s32[]{:T(128)}, f32[1,512]{1,0:T(1,128)S(1)}, f32[1,512]{1,0:T(1,128)S(1)}, f32[1,512,128]{2,1,0:T(8,128)S(1)}, s32[]{:T(128)}, /*index=5*/bf16[409...) while((s32[]{:T(128)}, f32[1,512]{1,0:T(1,128)S(1)}, ...), condition=%wide.region_9.10_spmd, body=%wide.region_6.9_spmd.sunk | while | flops 136710144 | bytes 4622503 | solution.py:117
  99.8 119.1 %all-gather.7.cloned.1.call-done = bf16[8,1024,256]{2,0,1:T(8,128)(2,1)} async-done(((bf16[8,16,256]{2,0,1:T(8,128)(2,1)}), bf16[8,1024,256]{2,0,1:T(8,128)(2,1)}) %all-gather.7.cloned.1.call-update) | async-done | bytes 4194320 | tf_op jit(solution)/shard_map/all_gather | solution.py:120
  218.9 3.3 constant_dynamic-slice_fusion.1
  222.2 1.3 copy.35
  224.6 2.4 convolution_convert_fusion
  227.1 1.0 fusion.71
  228.2 0.8 copy.34
  229.0 170.1 %all-gather.9.cloned.1.call-done = bf16[4096,2048]{1,0:T(8,128)(2,1)} async-done(((bf16[512,2048]{1,0:T(8,128)(2,1)}), bf16[4096,2048]{1,0:T(8,128)(2,1)}) %all-gather.9.cloned.1.call-update) | async-done | bytes 16777232 | tf_op jit(solution)/shard_map/all_gather | solution.py:70
  399.1 9.5 %reduce_sum.80 = bf16[512,2048]{1,0:T(8,128)(2,1)S(1)} reduce(bf16[8,512,2048]{2,1,0:T(8,128)(2,1)} %bitcast.131, bf16[]{:T(256)} %constant.99.clone.1), dimensions={0}, to_apply=%region_12.13 | reduce | flops 7340032 | bytes 18874370 | tf_op jit(solution)/shard_map/reduce_sum | solution.py:70
  408.7 0.9 fusion.47
  (117 shorter events, 17.3 us)
Async XLA Ops:
  7.2 217.5 %copy-start = (bf16[128,2048]{1,0:T(8,128)(2,1)S(1)}, bf16[128,2048]{1,0:T(8,128)(2,1)}, u32[]{:S(2)}) copy-start(bf16[128,2048]{1,0:T(8,128)(2,1)} %param.18) | copy-start | bytes 1572868
  7.2 51.8 %all-gather.5.cloned.1.call-start = ((), (), s32[]{:S(2)}) async-start(), calls=%async_computation | async-start | bytes 2359296 | tf_op jit(solution)/shard_map/all_gather | solution.py:74
  7.9 211.0 %all-gather.7.cloned.1.call-start = ((), (), s32[]{:S(2)}) async-start(), calls=%async_computation.1 | async-start | bytes 4259840 | tf_op jit(solution)/shard_map/all_gather | solution.py:120
  9.5 389.6 %all-gather.9.cloned.1.call-start = ((), (), s32[]{:S(2)}) async-start(), calls=%async_computation.2 | async-start | bytes 18874368 | tf_op jit(solution)/shard_map/all_gather | solution.py:70
  12.8 46.2 %copy-start.8 = (bf16[2048,128]{1,0:T(8,128)(2,1)S(1)}, bf16[2048,128]{1,0:T(8,128)(2,1)}, u32[]{:S(2)}) copy-start(bf16[2048,128]{1,0:T(8,128)(2,1)} %param.16) | copy-start | bytes 1572868
  58.9 2.6 copy-start.1
  58.9 2.6 copy-start.9
  61.5 1.0 copy-start.10
  62.6 15.7 %copy-start.14 = (f32[128]{0:T(128)S(1)}, f32[128]{0:T(128)}, u32[]{:S(2)}) copy-start(f32[128]{0:T(128)} %param.20) | copy-start | bytes 1540
  62.6 15.7 %copy-start.15 = (f32[128]{0:T(128)S(1)}, f32[128]{0:T(128)}, u32[]{:S(2)}) copy-start(f32[128]{0:T(128)} %param.19) | copy-start | bytes 1540
  63.5 19.8 %copy-start.2 = (f32[512,384]{0,1:T(8,128)}, f32[512,384]{0,1:T(8,128)S(1)}, u32[]{:S(2)}) copy-start(f32[512,384]{0,1:T(8,128)S(1)} %maximum_bitcast_fusion) | copy-start | bytes 2359300
  79.6 0.6 copy-start.4
  79.6 0.6 copy-start.6
  99.8 123.8 %copy-start.5 = (bf16[512,1,64]{0,2,1:T(8,128)(2,1)S(1)}, bf16[512,1,64]{0,2,1:T(8,128)(2,1)}, u32[]{:S(2)}) copy-start(bf16[512,1,64]{0,2,1:T(8,128)(2,1)} %copy-done.4) | copy-start | bytes 196612
  99.8 123.8 %copy-start.7 = (bf16[512,1,64]{0,2,1:T(8,128)(2,1)S(1)}, bf16[512,1,64]{0,2,1:T(8,128)(2,1)}, u32[]{:S(2)}) copy-start(bf16[512,1,64]{0,2,1:T(8,128)(2,1)} %copy-done.6) | copy-start | bytes 196612
  227.1 1.0 copy-start.11
  227.1 1.0 copy-start.12
  399.1 9.6 %copy-start.3 = (bf16[1,64,2048]{2,1,0:T(8,128)(2,1)S(1)}, bf16[1,64,2048]{2,1,0:T(8,128)(2,1)}, u32[]{:S(2)}) copy-start(bf16[1,64,2048]{2,1,0:T(8,128)(2,1)} %param.14) | copy-start | bytes 786436
  399.1 9.6 %copy-start.13 = (f32[2048]{0:T(1024)S(1)}, f32[2048]{0:T(1024)}, u32[]{:S(2)}) copy-start(f32[2048]{0:T(1024)} %param.21) | copy-start | bytes 24580
Sparse Core Ops, SparseCore 0:
  10.1 48.8 all-gather.4
  62.8 156.0 all-gather.6
  227.2 171.8 all-gather.8
